TPU v7x, 128 devices: a whole 4x4x4 slice. The times are simulated.
128 devices in a mesh: dp: 8 (over y, core), tensor: 16 (over z, x).
Axes of the slice: x: 4, y: 4, z: 4, core: 2. Of those that a mesh axis runs over, the one named last changes fastest.
Arguments:
- features: bfloat16 [1024, 4096], P('dp'), may hold values from -6 to 6
- enc_in: bfloat16 [4096, 2048], P(None, 'tensor'), may hold values from -0.09375 to 0.09375
- enc_out: bfloat16 [2048, 8192], P('tensor'), may hold values from -0.125 to 0.125
- noise: bfloat16 [1024, 4096], P('dp', 'tensor'), may hold values from -6 to 6
- in_weight: bfloat16 [4096, 16384], P('dp', 'tensor'), may hold values from -0.09375 to 0.09375
- out_weight: bfloat16 [4096, 16384], P('dp', 'tensor'), may hold values from -0.046875 to 0.046875
- probes: bfloat16 [2, 1024, 4096], P(None, 'dp'), may hold values from -6 to 6
Outputs:
- flowed: float32 [1024, 4096], P('dp', 'tensor')
- logdet: float32 [1024], P('dp')
All inputs are finite; a program needn't handle non-finite values.
Results may differ from a plain program's by a relative error of at most 0.017.
Values may be sent and summed in bfloat16 or wider, within the bound.
No kernel may reach another device: no remote copies, remote signals or barrier semaphores. Data moves between devices by JAX's collectives and lax.ppermute only.
A program may use at most 128 MiB of HBM per device.

v0:
```python
import jax
import jax.numpy as jnp
from jax import lax
from jax.sharding import PartitionSpec as P

L = 4096
PROBES = 2
TERMS = 3


def collect(partial_value):
    return lax.psum(partial_value.astype(jnp.bfloat16), "tensor")


def series(start, w_in, w_out, slope):
    start32 = start.astype(jnp.float32)
    current = start
    running = jnp.zeros((start.shape[1],), jnp.float32)
    for term_idx in range(TERMS):
        pulled = jnp.einsum("pbl,lh->pbh", current, w_out, preferred_element_type=jnp.float32)
        scaled = (pulled * slope[None]).astype(jnp.bfloat16)
        partial_value = jnp.einsum("pbh,lh->pbl", scaled, w_in, preferred_element_type=jnp.float32)
        current = collect(partial_value)
        coeff = (-1.0) ** term_idx / (term_idx + 1)
        running = running + coeff * jnp.sum(start32 * current.astype(jnp.float32), axis=(0, 2))
    return running


def local(features, enc_in, enc_out, noise, in_weight, out_weight, probes):
    hidden = jax.nn.silu(jnp.dot(features, enc_in, preferred_element_type=jnp.float32)).astype(
        jnp.bfloat16
    )
    partial_stats = jnp.dot(hidden, enc_out, preferred_element_type=jnp.float32)
    batch_rows = partial_stats.shape[0]
    moments = lax.psum_scatter(
        partial_stats.reshape(batch_rows, 2, L), "tensor", scatter_dimension=2, tiled=True
    )
    u_slice = (moments[:, 0] + jax.nn.softplus(moments[:, 1]) * noise.astype(jnp.float32)).astype(
        jnp.bfloat16
    )
    u_full = lax.all_gather(u_slice, "tensor", axis=1, tiled=True)
    w_in, w_out = (
        lax.all_gather(in_weight, "dp", axis=0, tiled=True),
        lax.all_gather(out_weight, "dp", axis=0, tiled=True),
    )
    pre_act = jnp.dot(u_full, w_in, preferred_element_type=jnp.float32)
    tanh_val = jnp.tanh(pre_act)
    squash = tanh_val.astype(jnp.bfloat16)
    slope = 1.0 - tanh_val * tanh_val
    branch_part = jnp.einsum("bh,lh->bl", squash, w_out, preferred_element_type=jnp.float32)
    flowed = u_slice.astype(jnp.float32) + lax.psum_scatter(
        branch_part.astype(jnp.bfloat16), "tensor", scatter_dimension=1, tiled=True
    ).astype(jnp.float32)
    running = series(probes, w_in, w_out, slope)
    logdet = running / PROBES
    return (flowed, logdet)


def solution(mesh):
    in_specs = (
        P("dp", None),
        P(None, "tensor"),
        P("tensor", None),
        P("dp", "tensor"),
        P("dp", "tensor"),
        P("dp", "tensor"),
        P(None, "dp", None),
    )
    out_specs = (P("dp", "tensor"), P("dp"))
    return jax.shard_map(local, mesh=mesh, in_specs=in_specs, out_specs=out_specs, check_vma=False)
```

profile of v0, /device:TPU:0, one launch (start us, length us, event | category | flops | bytes accessed | tf_op | source)
XLA Modules:
  0.0 636.0 jit_solution(1916886400833628591)
XLA Ops:
  7.2 0.0 copy-start
  7.2 0.0 reduce-scatter.3.cloned.1.call-start
  7.2 1.5 copy-done
  8.8 4.6 fusion.52
  13.4 4.6 copy.12
  17.9 0.0 copy-start.2
  17.9 0.0 reduce-scatter.3.cloned.1.call-update
  18.0 0.0 all-gather.4.cloned.1.call-start
  18.0 81.1 %reduce-scatter.3.cloned.1.call-done = f32[128,2,256]{2,0,1:T(8,128)} async-done(((f32[128,2,4096]{2,0,1:T(8,128)}), f32[128,2,256]{2,0,1:T(8,128)}) %reduce-scatter.3.cloned.1.call-update) | async-done | bytes 262160 | tf_op jit(solution)/shard_map/reduce_scatter | solution.py:35
  99.1 0.0 copy-done.2
  99.1 1.7 fusion.51
  100.8 0.0 all-gather.4.cloned.1.call-update
  100.8 0.0 all-gather.6.cloned.1.call-start
  100.9 0.7 all-gather.6.cloned.1.call-update
  101.5 0.0 all-gather.8.cloned.1.call-start
  101.6 0.5 all-gather.8.cloned.1.call-update
  102.1 0.0 all-reduce.4.cloned.1.call-start
  102.2 42.0 %all-gather.4.cloned.1.call-done = bf16[128,4096]{1,0:T(8,128)(2,1)} async-done(((bf16[128,256]{1,0:T(8,128)(2,1)}), bf16[128,4096]{1,0:T(8,128)(2,1)}) %all-gather.4.cloned.1.call-update) | async-done | bytes 1048592 | tf_op jit(solution)/shard_map/all_gather | solution.py:41
  144.2 50.7 %all-gather.6.cloned.1.call-done = bf16[4096,1024]{1,0:T(8,128)(2,1)} async-done(((bf16[512,1024]{1,0:T(8,128)(2,1)}), bf16[4096,1024]{1,0:T(8,128)(2,1)}) %all-gather.6.cloned.1.call-update) | async-done | bytes 8388624 | tf_op jit(solution)/shard_map/all_gather | solution.py:43
  194.9 5.0 multiply_subtract_fusion
  199.8 46.4 %all-gather.8.cloned.1.call-done = bf16[4096,1024]{1,0:T(8,128)(2,1)} async-done(((bf16[512,1024]{1,0:T(8,128)(2,1)}), bf16[4096,1024]{1,0:T(8,128)(2,1)}) %all-gather.8.cloned.1.call-update) | async-done | bytes 8388624 | tf_op jit(solution)/shard_map/all_gather | solution.py:44
  246.3 12.2 %fusion.12 = bf16[2,128,4096]{2,1,0:T(8,128)(2,1)} fusion(bf16[4096,1024]{1,0:T(8,128)(2,1)} %all-gather.6.cloned.1.call-done, bf16[2,128,4096]{2,1,0:T(8,128)(2,1)} %param.13, bf16[4096,1024]{1,0:T(8,128)(2,1)} %all-gather.8.cloned.1.call-done, f32[128,1024]{1,0:T(8,128)S(1)} %get-tuple-element.5), kind=kOutput, calls=%fused_computation.15 | convolution fusion | flops 4296540160 | bytes 21495808 | tf_op jit(solution)/shard_map/pbh,lh->pbl/dot_general | solution.py:22
  258.5 0.0 all-reduce.4.cloned.1.call-update
  258.5 0.0 all-reduce.6.cloned.1.call-start
  258.5 91.5 %all-reduce.4.cloned.1.call-done = bf16[2,128,4096]{2,1,0:T(8,128)(2,1)} async-done(((bf16[2,128,4096]{2,1,0:T(8,128)(2,1)}), bf16[2,128,4096]{2,1,0:T(8,128)(2,1)}) %all-reduce.4.cloned.1.call-update) | async-done | bytes 2097168 | tf_op jit(solution)/shard_map/psum | solution.py:12
  350.1 12.2 %fusion.15 = bf16[2,128,4096]{2,1,0:T(8,128)(2,1)} fusion(bf16[4096,1024]{1,0:T(8,128)(2,1)} %all-gather.6.cloned.1.call-done, bf16[2,128,4096]{2,1,0:T(8,128)(2,1)} %all-reduce.4.cloned.1.call-done, bf16[4096,1024]{1,0:T(8,128)(2,1)} %all-gather.8.cloned.1.call-done, f32[128,1024]{1,0:T(8,128)S(1)} %get-tuple-element.5), kind=kOutput, calls=%fused_computation.16 | convolution fusion | flops 4296540160 | bytes 21495808 | tf_op jit(solution)/shard_map/pbh,lh->pbl/dot_general | solution.py:22
  362.2 0.0 all-reduce.6.cloned.1.call-update
  362.3 0.2 reduce-scatter.5.cloned.1.call-start
  362.5 7.3 %convolution_convert_fusion = bf16[128,4096]{1,0:T(8,128)(2,1)} fusion(bf16[4096,1024]{1,0:T(8,128)(2,1)} %all-gather.8.cloned.1.call-done, bf16[128,1024]{1,0:T(8,128)(2,1)S(1)} %get-tuple-element.6), kind=kOutput, calls=%fused_computation.18 | convolution fusion | flops 1074266112 | bytes 9699328 | tf_op jit(solution)/shard_map/bh,lh->bl/dot_general | solution.py:50
  369.8 0.0 reduce-scatter.5.cloned.1.call-update
  369.8 0.0 copy-start.1
  369.8 0.0 all-reduce.8.cloned.1.call-start
  369.8 83.3 %all-reduce.6.cloned.1.call-done = bf16[2,128,4096]{2,1,0:T(8,128)(2,1)} async-done(((bf16[2,128,4096]{2,1,0:T(8,128)(2,1)}), bf16[2,128,4096]{2,1,0:T(8,128)(2,1)}) %all-reduce.6.cloned.1.call-update) | async-done | bytes 2097168 | tf_op jit(solution)/shard_map/psum | solution.py:12
  453.1 12.2 %fusion.18 = bf16[2,128,4096]{2,1,0:T(8,128)(2,1)} fusion(bf16[4096,1024]{1,0:T(8,128)(2,1)} %all-gather.6.cloned.1.call-done, bf16[2,128,4096]{2,1,0:T(8,128)(2,1)} %all-reduce.6.cloned.1.call-done, bf16[4096,1024]{1,0:T(8,128)(2,1)} %all-gather.8.cloned.1.call-done, f32[128,1024]{1,0:T(8,128)S(1)} %get-tuple-element.5), kind=kOutput, calls=%fused_computation.17 | convolution fusion | flops 4296540160 | bytes 21495808 | tf_op jit(solution)/shard_map/pbh,lh->pbl/dot_general | solution.py:22
  465.3 0.0 all-reduce.8.cloned.1.call-update
  465.4 64.4 %reduce-scatter.5.cloned.1.call-done = bf16[128,256]{1,0:T(8,128)(2,1)} async-done(((bf16[128,4096]{1,0:T(8,128)(2,1)}), bf16[128,256]{1,0:T(8,128)(2,1)}) %reduce-scatter.5.cloned.1.call-update) | async-done | bytes 65552 | tf_op jit(solution)/shard_map/reduce_scatter | solution.py:51
  529.8 0.0 copy-done.1
  529.8 1.5 convert_add_fusion
  531.3 92.4 %all-reduce.8.cloned.1.call-done = bf16[2,128,4096]{2,1,0:T(8,128)(2,1)} async-done(((bf16[2,128,4096]{2,1,0:T(8,128)(2,1)}), bf16[2,128,4096]{2,1,0:T(8,128)(2,1)}) %all-reduce.8.cloned.1.call-update) | async-done | bytes 2097168 | tf_op jit(solution)/shard_map/psum | solution.py:12
  623.7 5.0 fusion.22
  628.7 0.5 add_multiply_fusion
Async XLA Ops:
  7.2 1.6 copy-start
  7.2 91.9 %reduce-scatter.3.cloned.1.call-start = ((), (), s32[]{:S(2)}) async-start(), calls=%async_computation.2 | async-start | bytes 4456448 | tf_op jit(solution)/shard_map/reduce_scatter | solution.py:35
  17.9 81.2 %copy-start.2 = (bf16[128,256]{1,0:T(8,128)(2,1)S(1)}, bf16[128,256]{1,0:T(8,128)(2,1)}, u32[]{:S(2)}) copy-start(bf16[128,256]{1,0:T(8,128)(2,1)} %param.10) | copy-start | bytes 196612
  18.0 126.2 %all-gather.4.cloned.1.call-start = ((), (), s32[]{:S(2)}) async-start(), calls=%async_computation.3 | async-start | bytes 1114112 | tf_op jit(solution)/shard_map/all_gather | solution.py:41
  100.8 94.0 %all-gather.6.cloned.1.call-start = ((), (), s32[]{:S(2)}) async-start(), calls=%async_computation.4 | async-start | bytes 9437184 | tf_op jit(solution)/shard_map/all_gather | solution.py:43
  101.5 144.7 %all-gather.8.cloned.1.call-start = ((), (), s32[]{:S(2)}) async-start(), calls=%async_computation.5 | async-start | bytes 9437184 | tf_op jit(solution)/shard_map/all_gather | solution.py:44
  102.1 247.9 %all-reduce.4.cloned.1.call-start = ((), (), s32[]{:S(2)}) async-start(), calls=%async_computation.7 | async-start | bytes 4194304 | tf_op jit(solution)/shard_map/psum | solution.py:12
  258.5 194.7 %all-reduce.6.cloned.1.call-start = ((), (), s32[]{:S(2)}) async-start(), calls=%async_computation.8 | async-start | bytes 4194304 | tf_op jit(solution)/shard_map/psum | solution.py:12
  362.3 167.5 %reduce-scatter.5.cloned.1.call-start = ((), (), s32[]{:S(2)}) async-start(), calls=%async_computation.6 | async-start | bytes 1114112 | tf_op jit(solution)/shard_map/reduce_scatter | solution.py:51
  369.8 160.0 %copy-start.1 = (bf16[128,256]{1,0:T(8,128)(2,1)S(1)}, bf16[128,256]{1,0:T(8,128)(2,1)}, u32[]{:S(2)}) copy-start(bf16[128,256]{1,0:T(8,128)(2,1)} %fusion.51) | copy-start | bytes 196612
  369.8 253.9 %all-reduce.8.cloned.1.call-start = ((), (), s32[]{:S(2)}) async-start(), calls=%async_computation.9 | async-start | bytes 4194304 | tf_op jit(solution)/shard_map/psum | solution.py:12
Sparse Core Ops, SparseCore 0:
  18.1 80.9 reduce-scatter.2
  101.8 42.3 all-gather.3
  145.9 48.9 all-gather.5
  196.4 49.8 all-gather.7
  258.6 91.4 all-reduce.3
  362.4 90.7 all-reduce.5
  456.3 73.3 reduce-scatter.4
  533.1 90.5 all-reduce.7
where the time goes:
time: 636 us
  waiting for transfers between devices  553 us (87%)
  matrix products  53.4 us (8%)
  between operations  14.2 us (2%)
  other arithmetic  8.67 us (1%)
    psum x3, waiting for transfers between devices, collect(): return lax.psum(partial_value.astype(jnp.bfloat16), 'tensor')  267 us
    reduce_scatter x1, waiting for transfers between devices, local(): lax.psum_scatter(partial_stats.reshape(batch_rows, 2, L), 'tensor', scatt...  81.1 us
    reduce_scatter x1, waiting for transfers between devices, local(): lax.psum_scatter(branch_part.astype(jnp.bfloat16), 'tensor', scatter_dime...  64.4 us
    all_gather x1, waiting for transfers between devices, local(): lax.all_gather(in_weight, 'dp', axis=0, tiled=True)  50.7 us
    all_gather x1, waiting for transfers between devices, local(): lax.all_gather(out_weight, 'dp', axis=0, tiled=True)  46.4 us
    all_gather x1, waiting for transfers between devices, local(): u_full = lax.all_gather(u_slice, 'tensor', axis=1, tiled=True)  42 us
    dot_general x3, matrix products, series(): jnp.einsum('pbh,lh->pbl', scaled, w_in, preferred_element_type=jnp.float32)  36.6 us
  transfers between devices with their start and end apart: 8, of which 8 were waited for; matrix products, arithmetic and copies ran while one was open for 4% of the time, Pallas kernels for 0%

commit v1 on v0

--- a/solution.py
+++ b/solution.py
@@ -6,6 +6,22 @@
 L = 4096
 PROBES = 2
 TERMS = 3
+
+
+def ring_gather(x, axis, dim):
+    ways, here, hop = (lax.axis_size(axis), lax.axis_index(axis), x.shape[dim])
+    shape = [n * ways if d == dim else n for d, n in enumerate(x.shape)]
+    full = lax.dynamic_update_slice_in_dim(jnp.zeros(shape, x.dtype), x, here * hop, axis=dim)
+    going_up = going_down = x
+    for far in range(1, ways // 2 + 1):
+        going_up = lax.ppermute(going_up, axis, [(d, (d + 1) % ways) for d in range(ways)])
+        full = lax.dynamic_update_slice_in_dim(full, going_up, (here - far) % ways * hop, axis=dim)
+        if 2 * far < ways:
+            going_down = lax.ppermute(going_down, axis, [(d, (d - 1) % ways) for d in range(ways)])
+            full = lax.dynamic_update_slice_in_dim(
+                full, going_down, (here + far) % ways * hop, axis=dim
+            )
+    return full
 
 
 def collect(partial_value):
@@ -41,7 +57,7 @@
     u_full = lax.all_gather(u_slice, "tensor", axis=1, tiled=True)
     w_in, w_out = (
         lax.all_gather(in_weight, "dp", axis=0, tiled=True),
-        lax.all_gather(out_weight, "dp", axis=0, tiled=True),
+        ring_gather(out_weight, "dp", 0),
     )
     pre_act = jnp.dot(u_full, w_in, preferred_element_type=jnp.float32)
     tanh_val = jnp.tanh(pre_act)

time: 636 us -> 591 us (0.929)
  waiting for transfers between devices: 553 us -> 481 us
  local copies, waits for them, and re-layouts: 6.13 us -> 26.2 us
  starting transfers between devices: 0.5 us -> 7.43 us
    all_gather x1 -> x0, waiting for transfers between devices: 46.4 us -> none  [local(): lax.all_gather(out_weight, 'dp', axis=0, tiled=True)]
    ppermute x0 -> x7, waiting for transfers between devices: none -> 46.1 us  [the longest x4 46.1 us: ring_gather(): lax.ppermute(going_up, axis, [(d, (d + 1) % ways) for d in range(ways)])]
    all_gather x1, waiting for transfers between devices: 42 us -> 0.01 us  [local(): u_full = lax.all_gather(u_slice, 'tensor', axis=1, tiled=True)]
    all_gather x1, waiting for transfers between devices: 50.7 us -> 24.5 us  [local(): lax.all_gather(in_weight, 'dp', axis=0, tiled=True)]
    dynamic_update_slice x0 -> x8, local copies, waits for them, and re-layouts: none -> 13.5 us  [the longest x4 6.7 us: ring_gather(): lax.dynamic_update_slice_in_dim(full, going_up, (here - far) % ways * hop...]
    ppermute x0 -> x7, starting transfers between devices: none -> 6.97 us  [the longest x3 6.94 us: ring_gather(): lax.ppermute(going_down, axis, [(d, (d - 1) % ways) for d in range(ways)])]
  transfers between devices with their start and end apart: 8 -> 14, of which waited for: 8 -> 10; matrix products, arithmetic and copies ran while one was open for 4% -> 7% of each run, Pallas kernels for 0% -> 0%
where the time goes in v1:
time: 591 us
  waiting for transfers between devices  481 us (81%)
  matrix products  53.6 us (9%)
  local copies, waits for them, and re-layouts  26.2 us (4%)
  between operations  14.2 us (2%)
  other arithmetic  8.67 us (1%)
  starting transfers between devices  7.43 us (1%)
    psum x3, waiting for transfers between devices, collect(): return lax.psum(partial_value.astype(jnp.bfloat16), 'tensor')  264 us
    reduce_scatter x1, waiting for transfers between devices, local(): lax.psum_scatter(partial_stats.reshape(batch_rows, 2, L), 'tensor', scatt...  81.1 us
    reduce_scatter x1, waiting for transfers between devices, local(): lax.psum_scatter(branch_part.astype(jnp.bfloat16), 'tensor', scatter_dime...  64.3 us
    ppermute x4, waiting for transfers between devices, ring_gather(): lax.ppermute(going_up, axis, [(d, (d + 1) % ways) for d in range(ways)])  46.1 us
    dot_general x3, matrix products, series(): jnp.einsum('pbh,lh->pbl', scaled, w_in, preferred_element_type=jnp.float32)  36.7 us
    all_gather x1, waiting for transfers between devices, local(): lax.all_gather(in_weight, 'dp', axis=0, tiled=True)  24.5 us
  transfers between devices with their start and end apart: 14, of which 10 were waited for; matrix products, arithmetic and copies ran while one was open for 7% of the time, Pallas kernels for 0%

profile of v1, /device:TPU:0, one launch (start us, length us, event | category | flops | bytes accessed | tf_op | source)
XLA Modules:
  0.0 590.6 jit_solution(2403640525030720859)
XLA Ops:
  7.2 0.0 reduce-scatter.3.cloned.1.call-start
  7.2 1.5 copy-done
  8.8 4.6 fusion.55
  13.4 4.7 copy.12
  18.1 0.0 reduce-scatter.3.cloned.1.call-update
  18.1 0.0 all-gather.3.cloned.1.call-start
  18.2 81.1 %reduce-scatter.3.cloned.1.call-done = f32[128,2,256]{2,0,1:T(8,128)} async-done(((f32[128,2,4096]{2,0,1:T(8,128)}), f32[128,2,256]{2,0,1:T(8,128)}) %reduce-scatter.3.cloned.1.call-update) | async-done | bytes 262160 | tf_op jit(solution)/shard_map/reduce_scatter | solution.py:51
  99.2 1.7 fusion.54
  100.9 0.0 all-gather.3.cloned.1.call-update
  100.9 0.0 all-gather.5.cloned.1.call-start
  101.0 0.7 all-gather.5.cloned.1.call-update
  101.7 0.0 all-reduce.4.cloned.1.call-start
  101.7 0.0 collective-permute-start
  101.8 2.9 collective-permute-start.1
  104.7 12.5 %collective-permute-done = bf16[512,1024]{1,0:T(8,128)(2,1)S(1)} collective-permute-done((bf16[512,1024]{1,0:T(8,128)(2,1)S(1)}, bf16[512,1024]{1,0:T(8,128)(2,1)S(1)}, u32[]{:S(2)}, u32[]{:S(2)}) %collective-permute-start) | collective-permute-done | bytes 1048608 | tf_op jit(solution)/shard_map/ppermute | solution.py:17
  117.2 1.0 copy-done.2
  118.2 1.9 collective-permute-start.3
  120.2 12.5 %collective-permute-done.2 = bf16[512,1024]{1,0:T(8,128)(2,1)S(1)} collective-permute-done((bf16[512,1024]{1,0:T(8,128)(2,1)S(1)}, bf16[512,1024]{1,0:T(8,128)(2,1)S(1)}, u32[]{:S(2)}, u32[]{:S(2)}) %collective-permute-start.2) | collective-permute-done | bytes 1048608 | tf_op jit(solution)/shard_map/ppermute | solution.py:17
  132.6 1.0 copy-done.6
  133.6 2.1 collective-permute-start.5
  135.7 12.5 %collective-permute-done.4 = bf16[512,1024]{1,0:T(8,128)(2,1)} collective-permute-done((bf16[512,1024]{1,0:T(8,128)(2,1)S(1)}, bf16[512,1024]{1,0:T(8,128)(2,1)}, u32[]{:S(2)}, u32[]{:S(2)}) %collective-permute-start.4) | collective-permute-done | bytes 1048608 | tf_op jit(solution)/shard_map/ppermute | solution.py:17
  148.2 4.3 broadcast_in_dim.2
  152.5 1.1 constant_dynamic-update-slice_fusion.7
  153.6 1.1 constant_dynamic-update-slice_fusion.6
  154.7 1.0 constant_dynamic-update-slice_fusion.5
  155.7 1.0 constant_dynamic-update-slice_fusion.4
  156.8 2.4 constant_dynamic-update-slice_fusion.3
  159.2 2.3 constant_dynamic-update-slice_fusion.2
  161.4 2.3 constant_dynamic-update-slice_fusion.1
  163.7 8.7 %collective-permute-done.6 = bf16[512,1024]{1,0:T(8,128)(2,1)} collective-permute-done((bf16[512,1024]{1,0:T(8,128)(2,1)}, bf16[512,1024]{1,0:T(8,128)(2,1)}, u32[]{:S(2)}, u32[]{:S(2)}) %collective-permute-start.6) | collective-permute-done | bytes 1048608 | tf_op jit(solution)/shard_map/ppermute | solution.py:17
  172.4 2.3 constant_dynamic-update-slice_fusion
  174.8 24.5 %all-gather.5.cloned.1.call-done = bf16[4096,1024]{1,0:T(8,128)(2,1)} async-done(((bf16[512,1024]{1,0:T(8,128)(2,1)}), bf16[4096,1024]{1,0:T(8,128)(2,1)}) %all-gather.5.cloned.1.call-update) | async-done | bytes 8388624 | tf_op jit(solution)/shard_map/all_gather | solution.py:59
  199.3 5.0 multiply_subtract_fusion
  204.3 12.3 %fusion.12 = bf16[2,128,4096]{2,1,0:T(8,128)(2,1)} fusion(bf16[4096,1024]{1,0:T(8,128)(2,1)} %all-gather.5.cloned.1.call-done, bf16[2,128,4096]{2,1,0:T(8,128)(2,1)} %param.13, bf16[4096,1024]{1,0:T(8,128)(2,1)} %constant_dynamic-update-slice_fusion, f32[128,1024]{1,0:T(8,128)S(1)} %get-tuple-element.5), kind=kOutput, calls=%fused_computation.15 | convolution fusion | flops 4296540160 | bytes 21495808 | tf_op jit(solution)/shard_map/pbh,lh->pbl/dot_general | solution.py:38
  216.6 0.0 all-reduce.4.cloned.1.call-update
  216.6 0.2 all-reduce.6.cloned.1.call-start
  216.8 87.8 %all-reduce.4.cloned.1.call-done = bf16[2,128,4096]{2,1,0:T(8,128)(2,1)} async-done(((bf16[2,128,4096]{2,1,0:T(8,128)(2,1)}), bf16[2,128,4096]{2,1,0:T(8,128)(2,1)}) %all-reduce.4.cloned.1.call-update) | async-done | bytes 2097168 | tf_op jit(solution)/shard_map/psum | solution.py:28
  304.6 12.2 %fusion.15 = bf16[2,128,4096]{2,1,0:T(8,128)(2,1)} fusion(bf16[4096,1024]{1,0:T(8,128)(2,1)} %all-gather.5.cloned.1.call-done, bf16[2,128,4096]{2,1,0:T(8,128)(2,1)} %all-reduce.4.cloned.1.call-done, bf16[4096,1024]{1,0:T(8,128)(2,1)} %constant_dynamic-update-slice_fusion, f32[128,1024]{1,0:T(8,128)S(1)} %get-tuple-element.5), kind=kOutput, calls=%fused_computation.16 | convolution fusion | flops 4296540160 | bytes 21495808 | tf_op jit(solution)/shard_map/pbh,lh->pbl/dot_general | solution.py:38
  316.9 0.0 reduce-scatter.5.cloned.1.call-start
  316.9 7.3 %convolution_convert_fusion = bf16[128,4096]{1,0:T(8,128)(2,1)} fusion(bf16[4096,1024]{1,0:T(8,128)(2,1)} %constant_dynamic-update-slice_fusion, bf16[128,1024]{1,0:T(8,128)(2,1)S(1)} %get-tuple-element.6), kind=kOutput, calls=%fused_computation.18 | convolution fusion | flops 1074266112 | bytes 9699328 | tf_op jit(solution)/shard_map/bh,lh->bl/dot_general | solution.py:66
  324.2 0.0 all-reduce.8.cloned.1.call-start
  324.3 83.5 %all-reduce.6.cloned.1.call-done = bf16[2,128,4096]{2,1,0:T(8,128)(2,1)} async-done(((bf16[2,128,4096]{2,1,0:T(8,128)(2,1)}), bf16[2,128,4096]{2,1,0:T(8,128)(2,1)}) %all-reduce.6.cloned.1.call-update) | async-done | bytes 2097168 | tf_op jit(solution)/shard_map/psum | solution.py:28
  407.8 12.2 %fusion.18 = bf16[2,128,4096]{2,1,0:T(8,128)(2,1)} fusion(bf16[4096,1024]{1,0:T(8,128)(2,1)} %all-gather.5.cloned.1.call-done, bf16[2,128,4096]{2,1,0:T(8,128)(2,1)} %all-reduce.6.cloned.1.call-done, bf16[4096,1024]{1,0:T(8,128)(2,1)} %constant_dynamic-update-slice_fusion, f32[128,1024]{1,0:T(8,128)S(1)} %get-tuple-element.5), kind=kOutput, calls=%fused_computation.17 | convolution fusion | flops 4296540160 | bytes 21495808 | tf_op jit(solution)/shard_map/pbh,lh->pbl/dot_general | solution.py:38
  420.1 64.3 %reduce-scatter.5.cloned.1.call-done = bf16[128,256]{1,0:T(8,128)(2,1)} async-done(((bf16[128,4096]{1,0:T(8,128)(2,1)}), bf16[128,256]{1,0:T(8,128)(2,1)}) %reduce-scatter.5.cloned.1.call-update) | async-done | bytes 65552 | tf_op jit(solution)/shard_map/reduce_scatter | solution.py:67
  484.3 1.5 convert_add_fusion
  485.8 92.4 %all-reduce.8.cloned.1.call-done = bf16[2,128,4096]{2,1,0:T(8,128)(2,1)} async-done(((bf16[2,128,4096]{2,1,0:T(8,128)(2,1)}), bf16[2,128,4096]{2,1,0:T(8,128)(2,1)}) %all-reduce.8.cloned.1.call-update) | async-done | bytes 2097168 | tf_op jit(solution)/shard_map/psum | solution.py:28
  578.2 5.0 fusion.22
  583.2 0.5 add_multiply_fusion
  (27 shorter events, 0.1 us)
Async XLA Ops:
  7.2 1.6 copy-start
  7.2 92.0 %reduce-scatter.3.cloned.1.call-start = ((), (), s32[]{:S(2)}) async-start(), calls=%async_computation.2 | async-start | bytes 4456448 | tf_op jit(solution)/shard_map/reduce_scatter | solution.py:51
  13.4 85.9 %copy-start.9 = (bf16[128,256]{1,0:T(8,128)(2,1)S(1)}, bf16[128,256]{1,0:T(8,128)(2,1)}, u32[]{:S(2)}) copy-start(bf16[128,256]{1,0:T(8,128)(2,1)} %param.10) | copy-start | bytes 196612
  13.4 88.4 %copy-start.1 = (bf16[512,1024]{1,0:T(8,128)(2,1)S(1)}, bf16[512,1024]{1,0:T(8,128)(2,1)}, u32[]{:S(2)}) copy-start(bf16[512,1024]{1,0:T(8,128)(2,1)} %param.12) | copy-start | bytes 3145732
  18.1 156.7 %all-gather.3.cloned.1.call-start = ((), (), s32[]{:S(2)}) async-start(), calls=%async_computation.3 | async-start | bytes 1114112 | tf_op jit(solution)/shard_map/all_gather | solution.py:57
  100.9 98.4 %all-gather.5.cloned.1.call-start = ((), (), s32[]{:S(2)}) async-start(), calls=%async_computation.4 | async-start | bytes 9437184 | tf_op jit(solution)/shard_map/all_gather | solution.py:59
  101.7 202.9 %all-reduce.4.cloned.1.call-start = ((), (), s32[]{:S(2)}) async-start(), calls=%async_computation.6 | async-start | bytes 4194304 | tf_op jit(solution)/shard_map/psum | solution.py:28
  101.7 15.4 %collective-permute-start = (bf16[512,1024]{1,0:T(8,128)(2,1)S(1)}, bf16[512,1024]{1,0:T(8,128)(2,1)S(1)}, u32[]{:S(2)}, u32[]{:S(2)}) collective-permute-start(bf16[512,1024]{1,0:T(8,128)(2,1)S(1)} %copy-done.1), channel_id=1, source_target_pairs={{0,16},{16,32},{32,48},{48,64},{64,80},{80,96},{96,112},{112,0},{1... | collective-permute-start | bytes 3145736 | tf_op jit(solution)/shard_map/ppermute | solution.py:17
  101.8 15.4 %collective-permute-start.1 = (bf16[512,1024]{1,0:T(8,128)(2,1)S(1)}, bf16[512,1024]{1,0:T(8,128)(2,1)S(1)}, u32[]{:S(2)}, u32[]{:S(2)}) collective-permute-start(bf16[512,1024]{1,0:T(8,128)(2,1)S(1)} %copy-done.1), channel_id=1, source_target_pairs={{0,112},{16,0},{32,16},{48,32},{64,48},{80,64},{96,80},{112,96},{1... | collective-permute-start | bytes 3145736 | tf_op jit(solution)/shard_map/ppermute | solution.py:20
  117.2 1.0 copy-start.2
  117.2 15.4 %collective-permute-start.2 = (bf16[512,1024]{1,0:T(8,128)(2,1)S(1)}, bf16[512,1024]{1,0:T(8,128)(2,1)S(1)}, u32[]{:S(2)}, u32[]{:S(2)}) collective-permute-start(bf16[512,1024]{1,0:T(8,128)(2,1)S(1)} %collective-permute-done), channel_id=1, source_target_pairs={{0,16},{16,32},{32,48},{48,64},{64,80},{80,96},{96,112},{112,0},{1... | collective-permute-start | bytes 3145736 | tf_op jit(solution)/shard_map/ppermute | solution.py:17
  118.2 14.4 %copy-start.4 = (bf16[512,1024]{1,0:T(8,128)(2,1)}, bf16[512,1024]{1,0:T(8,128)(2,1)S(1)}, u32[]{:S(2)}) copy-start(bf16[512,1024]{1,0:T(8,128)(2,1)S(1)} %collective-permute-done.1) | copy-start | bytes 3145732
  118.2 14.4 %collective-permute-start.3 = (bf16[512,1024]{1,0:T(8,128)(2,1)S(1)}, bf16[512,1024]{1,0:T(8,128)(2,1)}, u32[]{:S(2)}, u32[]{:S(2)}) collective-permute-start(bf16[512,1024]{1,0:T(8,128)(2,1)S(1)} %collective-permute-done.1), channel_id=1, source_target_pairs={{0,112},{16,0},{32,16},{48,32},{64,48},{80,64},{96,80},{112,96},{1... | collective-permute-start | bytes 3145736 | tf_op jit(solution)/shard_map/ppermute | solution.py:20
  132.6 1.0 copy-start.6
  132.6 15.5 %collective-permute-start.4 = (bf16[512,1024]{1,0:T(8,128)(2,1)S(1)}, bf16[512,1024]{1,0:T(8,128)(2,1)}, u32[]{:S(2)}, u32[]{:S(2)}) collective-permute-start(bf16[512,1024]{1,0:T(8,128)(2,1)S(1)} %collective-permute-done.2), channel_id=1, source_target_pairs={{0,16},{16,32},{32,48},{48,64},{64,80},{80,96},{96,112},{112,0},{1... | collective-permute-start | bytes 3145736 | tf_op jit(solution)/shard_map/ppermute | solution.py:17
  133.6 27.8 %collective-permute-start.5 = (bf16[512,1024]{1,0:T(8,128)(2,1)}, bf16[512,1024]{1,0:T(8,128)(2,1)}, u32[]{:S(2)}, u32[]{:S(2)}) collective-permute-start(bf16[512,1024]{1,0:T(8,128)(2,1)} %collective-permute-done.3), channel_id=1, source_target_pairs={{0,112},{16,0},{32,16},{48,32},{64,48},{80,64},{96,80},{112,96},{1... | collective-permute-start | bytes 3145736 | tf_op jit(solution)/shard_map/ppermute | solution.py:20
  148.2 24.3 %collective-permute-start.6 = (bf16[512,1024]{1,0:T(8,128)(2,1)}, bf16[512,1024]{1,0:T(8,128)(2,1)}, u32[]{:S(2)}, u32[]{:S(2)}) collective-permute-start(bf16[512,1024]{1,0:T(8,128)(2,1)} %collective-permute-done.4), channel_id=1, source_target_pairs={{0,16},{16,32},{32,48},{48,64},{64,80},{80,96},{96,112},{112,0},{1... | collective-permute-start | bytes 3145736 | tf_op jit(solution)/shard_map/ppermute | solution.py:17
  148.2 5.5 copy-start.3
  148.2 6.5 %copy-start.5 = (bf16[512,1024]{1,0:T(8,128)(2,1)S(1)}, bf16[512,1024]{1,0:T(8,128)(2,1)}, u32[]{:S(2)}) copy-start(bf16[512,1024]{1,0:T(8,128)(2,1)} %copy-done.4) | copy-start | bytes 3145732
  148.2 7.6 %copy-start.7 = (bf16[512,1024]{1,0:T(8,128)(2,1)S(1)}, bf16[512,1024]{1,0:T(8,128)(2,1)}, u32[]{:S(2)}) copy-start(bf16[512,1024]{1,0:T(8,128)(2,1)} %copy-done.6) | copy-start | bytes 3145732
  216.6 191.2 %all-reduce.6.cloned.1.call-start = ((), (), s32[]{:S(2)}) async-start(), calls=%async_computation.7 | async-start | bytes 4194304 | tf_op jit(solution)/shard_map/psum | solution.py:28
  316.9 167.5 %reduce-scatter.5.cloned.1.call-start = ((), (), s32[]{:S(2)}) async-start(), calls=%async_computation.5 | async-start | bytes 1114112 | tf_op jit(solution)/shard_map/reduce_scatter | solution.py:67
  324.2 160.1 %copy-start.8 = (bf16[128,256]{1,0:T(8,128)(2,1)S(1)}, bf16[128,256]{1,0:T(8,128)(2,1)}, u32[]{:S(2)}) copy-start(bf16[128,256]{1,0:T(8,128)(2,1)} %fusion.54) | copy-start | bytes 196612
  324.2 254.0 %all-reduce.8.cloned.1.call-start = ((), (), s32[]{:S(2)}) async-start(), calls=%async_computation.8 | async-start | bytes 4194304 | tf_op jit(solution)/shard_map/psum | solution.py:28
Sparse Core Ops, SparseCore 0:
  18.2 80.9 reduce-scatter.2
  101.9 42.3 all-gather.2
  146.0 53.2 all-gather.4
  216.7 87.8 all-reduce.3
  317.0 90.7 all-reduce.5
  410.9 73.4 reduce-scatter.4
  487.7 90.5 all-reduce.7
